TPU v7x, 32 devices: a whole 2x2x4 slice. The times are simulated.
32 devices in a mesh: member: 2 (over y), vocab: 16 (over z, x, core).
Axes of the slice: x: 2, y: 2, z: 4, core: 2. Of those that a mesh axis runs over, the one named last changes fastest.
Arguments:
- hidden: bfloat16 [2, 512, 2048], P('member', None, 'vocab'), as said below
- norm_gain: bfloat16 [2, 2048], P('member', 'vocab'), may hold values from 0.5 to 1.5
- head: bfloat16 [2, 2048, 64128], P('member', None, 'vocab'), as said below
- pool_weight: float32 [2], P('member'), may hold values from 0.25 to 1
Outputs:
- log_probs: float32 [512, 64128], P('member', 'vocab')
- agreement: float32 [512], P('member')
Inputs may be any that keep to these rules, and one draw needn't show every extreme that they name: `hidden`: finite values; every member's row has a root mean square over its 2048 features between 0.1 and 100. `head`: finite values, each at most 60 in magnitude, so that a row's logits may reach about a thousand in magnitude.
All inputs are finite; a program needn't handle non-finite values.
Results may differ from a plain program's by a relative error of at most 0.00052.
Values may be sent and summed in bfloat16 or wider, within the bound.
No kernel may reach another device: no remote copies, remote signals or barrier semaphores. Data moves between devices by JAX's collectives and lax.ppermute only.
A program may use at most 128 MiB of HBM per device.

v0:
```python
import jax
import jax.numpy as jnp
from jax import lax
from jax.sharding import PartitionSpec as P

epsilon = 1e-05


def softmax_offset(values, first_pass):
    local_peak = jnp.max(values, axis=1)
    if first_pass:
        row_peak = lax.pmax(local_peak, "vocab")
        summed = lax.psum(jnp.sum(jnp.exp(values - row_peak[:, None]), axis=1), "vocab")
    else:
        row_peak = lax.pmax(local_peak, "vocab")
        summed = lax.psum(jnp.sum(jnp.exp(values - row_peak[:, None]), axis=1), "vocab")
    return row_peak + jnp.log(summed)


def on_device(hidden, norm_gain, head, pool_weight):
    states = hidden[0]
    weights = head[0]
    row_count = states.shape[0]
    narrowed = states.astype(jnp.float32)
    squares = lax.psum(jnp.sum(narrowed * narrowed, axis=1), "vocab")
    width_all = narrowed.shape[1] * lax.axis_size("vocab")
    scaling = lax.rsqrt(squares / width_all + epsilon)[:, None]
    normed = (narrowed * scaling * norm_gain.astype(jnp.float32)).astype(jnp.bfloat16)
    logits = jnp.dot(
        lax.all_gather(normed, "vocab", axis=1, tiled=True),
        weights,
        preferred_element_type=jnp.float32,
    )
    member_lse = softmax_offset(logits, True)
    weighted = pool_weight[0] * (logits - member_lse[:, None])
    share = row_count // lax.axis_size("member")
    pooled_all = lax.psum(weighted, "member")
    kept_rows = lax.dynamic_slice_in_dim(pooled_all, lax.axis_index("member") * share, share, 0)
    agreement = softmax_offset(kept_rows, False)
    return (kept_rows - agreement[:, None], agreement)


def solution(mesh):
    in_specs = (
        P("member", None, "vocab"),
        P("member", "vocab"),
        P("member", None, "vocab"),
        P("member"),
    )
    out_specs = (P("member", "vocab"), P("member"))
    return jax.shard_map(
        on_device, mesh=mesh, in_specs=in_specs, out_specs=out_specs, check_vma=False
    )
```

profile of v0, /device:TPU:0, one launch (start us, length us, event | category | flops | bytes accessed | tf_op | source)
XLA Modules:
  0.0 442.6 jit_solution(5408095204166017930)
XLA Ops:
  7.2 0.0 all-gather.2.cloned.1.call-start
  7.2 1.1 fusion.2
  8.3 34.9 %psum.28 = f32[512]{0:T(512)S(1)} all-reduce(f32[512]{0:T(512)S(1)} %fusion.2), channel_id=1, replica_groups=mesh['member'=2,'vocab'=16] {'vocab'}, use_global_device_ids=true, to_apply=%region_1.0 | all-reduce | flops 512 | bytes 4096 | tf_op jit(solution)/shard_map/psum | solution.py:25
  43.2 0.7 bitcast_convert_fusion
  43.8 1.7 fusion.4
  45.5 0.0 all-gather.2.cloned.1.call-update
  45.6 0.0 all-reduce.2.cloned.1.call-start
  46.3 37.9 %all-gather.2.cloned.1.call-done = bf16[512,2048]{1,0:T(8,128)(2,1)} async-done(((bf16[512,128]{1,0:T(8,128)(2,1)}), bf16[512,2048]{1,0:T(8,128)(2,1)}) %all-gather.2.cloned.1.call-update) | async-done | bytes 2097168 | tf_op jit(solution)/shard_map/all_gather | solution.py:30
  84.2 14.4 %fusion.5 = (f32[512]{0:T(512)S(1)}, f32[512,4008]{0,1:T(8,128)}) fusion(bf16[512,2048]{1,0:T(8,128)(2,1)} %all-gather.2.cloned.1.call-done, bf16[1,2048,4008]{1,2,0:T(8,128)(2,1)} %param.6), kind=kOutput, calls=%fused_computation.16 | convolution fusion | flops 8407436800 | bytes 26724352 | tf_op jit(solution)/shard_map/dot_general | solution.py:29
  98.6 31.6 %pmax.14 = f32[512]{0:T(512)S(1)} all-reduce(f32[512]{0:T(512)S(1)} %get-tuple-element.2), channel_id=1, replica_groups=mesh['member'=2,'vocab'=16] {'vocab'}, use_global_device_ids=true, to_apply=%region_3.0 | all-reduce | flops 512 | bytes 4096 | tf_op jit(solution)/shard_map/pmax | solution.py:12
  130.1 4.5 %exponential_reduce_fusion = f32[512]{0:T(512)S(1)} fusion(f32[512,4008]{0,1:T(8,128)} %get-tuple-element.3, f32[512]{0:T(512)S(1)} %pmax.14), kind=kLoop, calls=%fused_computation.3 | loop fusion | flops 4103680 | bytes 8212480 | tf_op jit(solution)/shard_map/reduce_sum | solution.py:13
  134.6 29.5 %psum.29 = f32[512]{0:T(512)S(1)} all-reduce(f32[512]{0:T(512)S(1)} %exponential_reduce_fusion), channel_id=1, replica_groups=mesh['member'=2,'vocab'=16] {'vocab'}, use_global_device_ids=true, to_apply=%region_5.0 | all-reduce | flops 512 | bytes 4096 | tf_op jit(solution)/shard_map/psum | solution.py:13
  164.1 7.6 %subtract_multiply_fusion = f32[512,4008]{0,1:T(8,128)} fusion(f32[512,4008]{0,1:T(8,128)} %get-tuple-element.3, f32[512]{0:T(512)S(1)} %log_add_fusion, f32[]{:T(128)} %bitcast.14), kind=kLoop, calls=%fused_computation.2 | loop fusion | flops 4104192 | bytes 16418820 | tf_op jit(solution)/shard_map/mul | solution.py:35
  171.7 0.0 all-reduce.2.cloned.1.call-update
  171.7 191.5 %all-reduce.2.cloned.1.call-done = f32[512,4008]{0,1:T(8,128)} async-done(((f32[512,4008]{0,1:T(8,128)}), f32[512,4008]{0,1:T(8,128)}) %all-reduce.2.cloned.1.call-update) | async-done | bytes 8208400 | tf_op jit(solution)/shard_map/psum | solution.py:37
  363.2 2.7 dynamic-slice_reduce_fusion
  365.9 33.1 %pmax.15 = f32[256]{0:T(256)S(1)} all-reduce(f32[256]{0:T(256)S(1)} %dynamic-slice_reduce_fusion), channel_id=1, replica_groups=mesh['member'=2,'vocab'=16] {'vocab'}, use_global_device_ids=true, to_apply=%region_8.0 | all-reduce | flops 256 | bytes 2048 | tf_op jit(solution)/shard_map/pmax | solution.py:15
  399.1 2.8 exponential_reduce_fusion.1
  401.9 29.5 %psum.31 = f32[256]{0:T(256)S(1)} all-reduce(f32[256]{0:T(256)S(1)} %exponential_reduce_fusion.1), channel_id=1, replica_groups=mesh['member'=2,'vocab'=16] {'vocab'}, use_global_device_ids=true, to_apply=%region_10.0 | all-reduce | flops 256 | bytes 2048 | tf_op jit(solution)/shard_map/psum | solution.py:16
  431.4 0.0 copy-start
  431.4 4.4 dynamic-slice_subtract_fusion
  435.8 0.0 copy-done
  (3 shorter events, 0.0 us)
Async XLA Ops:
  7.2 77.0 %all-gather.2.cloned.1.call-start = ((), (), s32[]{:S(2)}) async-start(), calls=%async_computation | async-start | bytes 2228224 | tf_op jit(solution)/shard_map/all_gather | solution.py:30
  45.6 317.7 %all-reduce.2.cloned.1.call-start = ((), (), s32[]{:S(2)}) async-start(), calls=%async_computation.1 | async-start | bytes 16416768 | tf_op jit(solution)/shard_map/psum | solution.py:37
  431.4 4.4 copy-start
Sparse Core Ops, SparseCore 0:
  45.7 38.4 all-gather.1
  171.8 191.3 all-reduce.1
where the time goes:
time: 443 us
  waiting for transfers between devices  229 us (52%)
  blocking collectives  159 us (36%)
  other arithmetic  25.4 us (6%)
  between operations  14.7 us (3%)
  matrix products  14.4 us (3%)
    psum x1, waiting for transfers between devices, on_device(): pooled_all = lax.psum(weighted, 'member')  192 us
    pmax x2, blocking collectives, softmax_offset(): row_peak = lax.pmax(local_peak, 'vocab')  64.7 us
    psum x2, blocking collectives, softmax_offset(): lax.psum(jnp.sum(jnp.exp(values - row_peak[:, None]), axis=1), 'vocab')  59 us
    all_gather x1, waiting for transfers between devices, on_device(): lax.all_gather(normed, 'vocab', axis=1, tiled=True)  37.9 us
    psum x1, blocking collectives, on_device(): squares = lax.psum(jnp.sum(narrowed * narrowed, axis=1), 'vocab')  34.9 us
    dot_general x1, matrix products, on_device(): jnp.dot(lax.all_gather(normed, 'vocab', axis=1, tiled=True), weights, pre...  14.4 us
  transfers between devices with their start and end apart: 2, of which 2 were waited for; matrix products, arithmetic and copies ran while one was open for 0% of the time, Pallas kernels for 0%

commit v1 on v0

--- a/solution.py
+++ b/solution.py
@@ -4,6 +4,39 @@
 from jax.sharding import PartitionSpec as P
 
 epsilon = 1e-05
+
+
+def _show_values(local_block, dim_at):
+    local_block = jnp.moveaxis(local_block, 0, dim_at)
+    earlier = local_block.shape
+    w1 = local_block.reshape(
+        *earlier[:dim_at], earlier[dim_at] * earlier[dim_at + 1], *earlier[dim_at + 2 :]
+    )
+    return w1
+
+
+def list_the_things(xx, which_axis):
+    arr_next = lax.axis_size(which_axis)
+    step_out = lax.axis_index(which_axis)
+    outer, shaped = (arr_next, step_out)
+    part_next, front = (xx[None], 1)
+    while front < outer:
+        base_arr = range(outer)
+        work_now = map(lambda to_i: (to_i, to_i ^ front), base_arr)
+        y2 = list(work_now)
+        piece_next = lax.ppermute(part_next, which_axis, y2)
+        all_rows = shaped & front == 0
+        e_now = jnp.where(all_rows, part_next, piece_next)
+        e_next = jnp.where(all_rows, piece_next, part_next)
+        part_next = jnp.concatenate([e_now, e_next])
+        front *= 2
+    return part_next
+
+
+def fit_squares(obj, patch, at_axis):
+    z2 = list_the_things(obj, patch)
+    w_next = _show_values(z2, at_axis)
+    return w_next
 
 
 def softmax_offset(values, first_pass):
@@ -26,11 +59,7 @@
     width_all = narrowed.shape[1] * lax.axis_size("vocab")
     scaling = lax.rsqrt(squares / width_all + epsilon)[:, None]
     normed = (narrowed * scaling * norm_gain.astype(jnp.float32)).astype(jnp.bfloat16)
-    logits = jnp.dot(
-        lax.all_gather(normed, "vocab", axis=1, tiled=True),
-        weights,
-        preferred_element_type=jnp.float32,
-    )
+    logits = jnp.dot(fit_squares(normed, "vocab", 1), weights, preferred_element_type=jnp.float32)
     member_lse = softmax_offset(logits, True)
     weighted = pool_weight[0] * (logits - member_lse[:, None])
     share = row_count // lax.axis_size("member")

time: 443 us -> 471 us (1.063)
  waiting for transfers between devices: 229 us -> 261 us
    ppermute x0 -> x4, waiting for transfers between devices: none -> 69 us  [list_the_things(): piece_next = lax.ppermute(part_next, which_axis, y2)]
    all_gather x1 -> x0, waiting for transfers between devices: 37.9 us -> none  [on_device(): lax.all_gather(normed, 'vocab', axis=1, tiled=True)]
  transfers between devices with their start and end apart: 2 -> 5, of which waited for: 2 -> 5; matrix products, arithmetic and copies ran while one was open for 0% -> 0% of each run, Pallas kernels for 0% -> 0%
where the time goes in v1:
time: 471 us
  waiting for transfers between devices  261 us (55%)
  blocking collectives  156 us (33%)
  other arithmetic  23.5 us (5%)
  between operations  14.8 us (3%)
  matrix products  14.1 us (3%)
    psum x1, waiting for transfers between devices, on_device(): pooled_all = lax.psum(weighted, 'member')  192 us
    ppermute x4, waiting for transfers between devices, list_the_things(): piece_next = lax.ppermute(part_next, which_axis, y2)  69 us
    pmax x2, blocking collectives, softmax_offset(): row_peak = lax.pmax(local_peak, 'vocab')  62.6 us
    psum x2, blocking collectives, softmax_offset(): lax.psum(jnp.sum(jnp.exp(values - row_peak[:, None]), axis=1), 'vocab')  59 us
    psum x1, blocking collectives, on_device(): squares = lax.psum(jnp.sum(narrowed * narrowed, axis=1), 'vocab')  34.9 us
    dot_general x1, matrix products, on_device(): jnp.dot(fit_squares(normed, 'vocab', 1), weights, preferred_element_type=...  14.1 us
  transfers between devices with their start and end apart: 5, of which 5 were waited for; matrix products, arithmetic and copies ran while one was open for 0% of the time, Pallas kernels for 0%

profile of v1, /device:TPU:0, one launch (start us, length us, event | category | flops | bytes accessed | tf_op | source)
XLA Modules:
  0.0 470.8 jit_solution(7198621762765088229)
XLA Ops:
  7.2 0.0 all-reduce.2.cloned.1.call-start
  7.2 0.7 bitcast_convert_fusion
  7.9 1.0 copy.6
  8.9 34.9 %psum.28 = f32[512]{0:T(512)S(1)} all-reduce(f32[512]{0:T(512)S(1)} %fusion.2), channel_id=1, replica_groups=mesh['member'=2,'vocab'=16] {'vocab'}, use_global_device_ids=true, to_apply=%region_1.0 | all-reduce | flops 512 | bytes 4096 | tf_op jit(solution)/shard_map/psum | solution.py:58
  43.8 0.1 fusion.4
  43.9 0.1 collective-permute-start
  44.0 1.3 collective-permute-done
  45.3 0.1 broadcast_select_fusion.7
  45.5 0.1 collective-permute-start.1
  45.6 8.3 %collective-permute-done.1 = bf16[2,512,128]{1,2,0:T(8,128)(2,1)S(1)} collective-permute-done((bf16[2,512,128]{1,2,0:T(8,128)(2,1)S(1)}, bf16[2,512,128]{1,2,0:T(8,128)(2,1)S(1)}, u32[]{:S(2)}, u32[]{:S(2)}) %collective-permute-start.1) | collective-permute-done | bytes 262176 | tf_op jit(solution)/shard_map/ppermute | solution.py:27
  54.0 0.1 collective-permute-start.2
  54.1 13.1 %collective-permute-done.2 = bf16[4,512,128]{1,2,0:T(8,128)(2,1)S(1)} collective-permute-done((bf16[4,512,128]{1,2,0:T(8,128)(2,1)S(1)}, bf16[4,512,128]{1,2,0:T(8,128)(2,1)S(1)}, u32[]{:S(2)}, u32[]{:S(2)}) %collective-permute-start.2) | collective-permute-done | bytes 524320 | tf_op jit(solution)/shard_map/ppermute | solution.py:27
  67.2 0.1 broadcast_select_fusion.3
  67.3 0.1 pad_maximum_fusion.1
  67.4 0.1 collective-permute-start.3
  68.2 46.2 %collective-permute-done.3 = bf16[8,512,128]{1,2,0:T(8,128)(2,1)S(1)} collective-permute-done((bf16[8,512,128]{1,2,0:T(8,128)(2,1)S(1)}, bf16[8,512,128]{1,2,0:T(8,128)(2,1)S(1)}, u32[]{:S(2)}, u32[]{:S(2)}) %collective-permute-start.3) | collective-permute-done | bytes 1048608 | tf_op jit(solution)/shard_map/ppermute | solution.py:27
  114.3 0.1 broadcast_select_fusion.1
  114.5 0.2 pad_maximum_fusion
  114.7 14.1 %fusion.5 = (f32[512]{0:T(512)S(1)}, f32[512,4008]{0,1:T(8,128)}) fusion(bf16[512,2048]{0,1:T(8,128)(2,1)S(1)} %bitcast.14, bf16[1,2048,4008]{1,2,0:T(8,128)(2,1)} %param.6), kind=kOutput, calls=%fused_computation.28 | convolution fusion | flops 8407436800 | bytes 26724352 | tf_op jit(solution)/shard_map/dot_general | solution.py:62
  128.8 29.5 %pmax.14 = f32[512]{0:T(512)S(1)} all-reduce(f32[512]{0:T(512)S(1)} %get-tuple-element.10), channel_id=1, replica_groups=mesh['member'=2,'vocab'=16] {'vocab'}, use_global_device_ids=true, to_apply=%region_3.4 | all-reduce | flops 512 | bytes 4096 | tf_op jit(solution)/shard_map/pmax | solution.py:45
  158.3 4.5 exponential_reduce_fusion
  162.7 29.5 %psum.29 = f32[512]{0:T(512)S(1)} all-reduce(f32[512]{0:T(512)S(1)} %exponential_reduce_fusion), channel_id=1, replica_groups=mesh['member'=2,'vocab'=16] {'vocab'}, use_global_device_ids=true, to_apply=%region_5.6 | all-reduce | flops 512 | bytes 4096 | tf_op jit(solution)/shard_map/psum | solution.py:46
  192.2 7.6 %subtract_multiply_fusion = f32[512,4008]{0,1:T(8,128)} fusion(f32[512,4008]{0,1:T(8,128)} %get-tuple-element.11, f32[512]{0:T(512)S(1)} %log_add_fusion, f32[]{:T(128)} %bitcast.13), kind=kLoop, calls=%fused_computation.2 | loop fusion | flops 4104192 | bytes 16418820 | tf_op jit(solution)/shard_map/mul | solution.py:64
  199.8 0.0 all-reduce.2.cloned.1.call-update
  199.8 191.6 %all-reduce.2.cloned.1.call-done = f32[512,4008]{0,1:T(8,128)} async-done(((f32[512,4008]{0,1:T(8,128)}), f32[512,4008]{0,1:T(8,128)}) %all-reduce.2.cloned.1.call-update) | async-done | bytes 8208400 | tf_op jit(solution)/shard_map/psum | solution.py:66
  391.4 2.7 dynamic-slice_reduce_fusion
  394.1 33.1 %pmax.15 = f32[256]{0:T(256)S(1)} all-reduce(f32[256]{0:T(256)S(1)} %dynamic-slice_reduce_fusion), channel_id=1, replica_groups=mesh['member'=2,'vocab'=16] {'vocab'}, use_global_device_ids=true, to_apply=%region_8.9 | all-reduce | flops 256 | bytes 2048 | tf_op jit(solution)/shard_map/pmax | solution.py:48
  427.2 2.8 exponential_reduce_fusion.1
  430.0 29.5 %psum.31 = f32[256]{0:T(256)S(1)} all-reduce(f32[256]{0:T(256)S(1)} %exponential_reduce_fusion.1), channel_id=1, replica_groups=mesh['member'=2,'vocab'=16] {'vocab'}, use_global_device_ids=true, to_apply=%region_10.11 | all-reduce | flops 256 | bytes 2048 | tf_op jit(solution)/shard_map/psum | solution.py:49
  459.5 0.0 copy-start
  459.5 4.4 dynamic-slice_subtract_fusion
  463.9 0.0 copy-done
  (7 shorter events, 0.2 us)
Async XLA Ops:
  7.2 384.2 %all-reduce.2.cloned.1.call-start = ((), (), s32[]{:S(2)}) async-start(), calls=%async_computation | async-start | bytes 16416768 | tf_op jit(solution)/shard_map/psum | solution.py:66
  43.9 1.4 collective-permute-start
  45.5 8.4 %collective-permute-start.1 = (bf16[2,512,128]{1,2,0:T(8,128)(2,1)S(1)}, bf16[2,512,128]{1,2,0:T(8,128)(2,1)S(1)}, u32[]{:S(2)}, u32[]{:S(2)}) collective-permute-start(bf16[2,512,128]{1,2,0:T(8,128)(2,1)S(1)} %pad_maximum_fusion.3), channel_id=1, source_target_pairs={{0,2},{1,3},{2,0},{3,1},{4,6},{5,7},{6,4},{7,5},{8,10},{9,11},{10,... | collective-permute-start | bytes 786440 | tf_op jit(solution)/shard_map/ppermute | solution.py:27
  54.0 13.2 %collective-permute-start.2 = (bf16[4,512,128]{1,2,0:T(8,128)(2,1)S(1)}, bf16[4,512,128]{1,2,0:T(8,128)(2,1)S(1)}, u32[]{:S(2)}, u32[]{:S(2)}) collective-permute-start(bf16[4,512,128]{1,2,0:T(8,128)(2,1)S(1)} %pad_maximum_fusion.2), channel_id=1, source_target_pairs={{0,4},{1,5},{2,6},{3,7},{4,0},{5,1},{6,2},{7,3},{8,12},{9,13},{10,... | collective-permute-start | bytes 1572872 | tf_op jit(solution)/shard_map/ppermute | solution.py:27
  67.4 46.9 %collective-permute-start.3 = (bf16[8,512,128]{1,2,0:T(8,128)(2,1)S(1)}, bf16[8,512,128]{1,2,0:T(8,128)(2,1)S(1)}, u32[]{:S(2)}, u32[]{:S(2)}) collective-permute-start(bf16[8,512,128]{1,2,0:T(8,128)(2,1)S(1)} %pad_maximum_fusion.1), channel_id=1, source_target_pairs={{0,8},{1,9},{2,10},{3,11},{4,12},{5,13},{6,14},{7,15},{8,0},{9,1},... | collective-permute-start | bytes 3145736 | tf_op jit(solution)/shard_map/ppermute | solution.py:27
  459.5 4.4 copy-start
Sparse Core Ops, SparseCore 0:
  199.9 191.3 all-reduce.1
